TPU v7x, 128 devices: a whole 4x4x4 slice. The times are simulated.
128 devices in a mesh: row: 4 (over y), vocab: 32 (over z, x, core).
Axes of the slice: x: 4, y: 4, z: 4, core: 2. Of those that a mesh axis runs over, the one named last changes fastest.
Arguments:
- tokens: bfloat16 [1280, 7168], P(('row', 'vocab')), may hold values from -60 to 60
- norm_gain: float32 [7168], replicated, may hold values from 0.5 to 1.5
- router: bfloat16 [7168, 32], replicated, may hold values from -0.0625 to 0.0625
- routes: int32 [1280, 8], P(('row', 'vocab')), may hold values from 0 to 31, all different within a row; in each aligned block of 10 rows (0 to 9, 10 to 19, ...) at most 3 rows name the same one
- w_gate: bfloat16 [32, 7168, 1024], P('vocab', None, 'row'), may hold values from -0.0625 to 0.0625
- w_up: bfloat16 [32, 7168, 1024], P('vocab', None, 'row'), may hold values from -0.0625 to 0.0625
- w_down: bfloat16 [32, 1024, 7168], P('vocab', 'row'), may hold values from -0.1875 to 0.1875
- head_gain: float32 [7168], replicated, may hold values from 0.5 to 1.5
- head: bfloat16 [65536, 7168], P(('row', 'vocab')), may hold values from -0.18 to 0.18
- draft_logits: bfloat16 [256, 4, 65536], P(None, None, ('row', 'vocab')), may hold values from -18 to 235
- draft_tokens: int32 [256, 4], replicated, may hold values from 0 to 65535
- reject_pos: int32 [256], replicated, may hold values from 0 to 4
Outputs:
- residual: float32 [256, 65536], P(None, ('row', 'vocab'))
- accept: float32 [256, 4], replicated
Inputs may be any that keep to these rules, and one draw needn't show every extreme that they name: `routes`: each row names 8 different experts. Among the rows of one device no expert is named more than 3 times, and some device's rows name some expert exactly 3 times.
All inputs are finite; a program needn't handle non-finite values.
Results may differ from a plain program's by a relative error of at most 0.012.
Values may be sent and summed in bfloat16 or wider, within the bound.
No kernel may reach another device: no remote copies, remote signals or barrier semaphores. Data moves between devices by JAX's collectives and lax.ppermute only.
A program may use at most 256 MiB of HBM per device.

v0:
```python
import jax
import jax.numpy as jnp
import numpy as np
from jax import lax
from jax.sharding import Mesh
from jax.sharding import PartitionSpec as P

V = 65536
DRAFTS = 4
VOCAB_AXES = ("vz", "vx", "core")
ALL_AXES = ("row",) + VOCAB_AXES
RING_ORDER = ("core", "vx", "vz", "row")


def rms_norm(values, gain):
    return values * lax.rsqrt(jnp.mean(values * values, axis=-1, keepdims=True) + 1e-06) * gain


def tree_psum(values):
    for axis in RING_ORDER:
        values = lax.psum(values, axis)
    return values


def tree_pmax(values):
    for axis in RING_ORDER:
        values = lax.pmax(values, axis)
    return values


def body(
    tokens,
    norm_gain,
    router,
    routes,
    w_gate,
    w_up,
    w_down,
    head_gain,
    head,
    draft_logits,
    draft_tokens,
    reject_pos,
):
    vocab_count = 1
    for axis in VOCAB_AXES:
        vocab_count *= lax.axis_size(axis)
    row_count = lax.axis_size("row")
    rows_dev = tokens.shape[0]
    model_width = tokens.shape[1]
    top_k = routes.shape[1]
    experts = w_gate.shape[0] * vocab_count
    capacity = min(rows_dev, (rows_dev * top_k + experts - 1) // experts)
    local_vocab = head.shape[0]
    requests = draft_tokens.shape[0]
    slot_total = DRAFTS + 1
    offset = lax.axis_index(ALL_AXES) * local_vocab
    local_ids = draft_tokens - offset
    id_match = jnp.arange(local_vocab, dtype=jnp.int32)[None, None, :] == local_ids[:, :, None]
    draft_vals = draft_logits.astype(jnp.float32)
    top_draft = tree_pmax(jnp.max(draft_vals, axis=-1))
    draft_exp = jnp.exp(draft_vals - top_draft[:, :, None])
    sum_draft, pick_d = tree_psum(
        (jnp.sum(draft_exp, axis=-1), jnp.sum(jnp.where(id_match, draft_vals, 0.0), axis=-1))
    )
    resid_in = tokens.astype(jnp.float32)
    normed = rms_norm(resid_in, norm_gain).astype(jnp.bfloat16)
    scores = jax.nn.sigmoid(jnp.dot(normed, router, preferred_element_type=jnp.float32))
    member = routes[:, :, None] == jnp.arange(experts, dtype=jnp.int32)[None, None, :]
    chosen = jnp.any(member, axis=1)
    chosen_int = chosen.astype(jnp.int32)
    picked = chosen.astype(jnp.float32) * scores
    weights = 2.5 * picked / jnp.sum(picked, axis=1, keepdims=True)
    earlier = jnp.cumsum(chosen_int, axis=0) - chosen_int
    slot_ids = jnp.arange(capacity, dtype=jnp.int32)[None, :, None]
    selector = ((earlier.T[:, None, :] == slot_ids) & chosen.T[:, None, :]).astype(jnp.float32)
    send_buffer = jnp.einsum(
        "esr,rd->sed", selector.astype(jnp.bfloat16), normed, preferred_element_type=jnp.float32
    ).astype(jnp.bfloat16)
    gate_w = w_gate[0]
    up_w = w_up[0]
    down_w = w_down[0]
    received = lax.all_to_all(send_buffer, VOCAB_AXES, split_axis=1, concat_axis=1, tiled=True)
    shard_piece = lax.all_gather(received, "row", axis=1, tiled=True)
    flat_rows = shard_piece.reshape(-1, model_width)
    gate_out = jnp.dot(flat_rows, gate_w, preferred_element_type=jnp.float32)
    up_out = jnp.dot(flat_rows, up_w, preferred_element_type=jnp.float32)
    hidden = (jax.nn.silu(gate_out) * up_out).astype(jnp.bfloat16)
    down_out = jnp.dot(hidden, down_w, preferred_element_type=jnp.float32).astype(jnp.bfloat16)
    summed = lax.psum_scatter(
        down_out.reshape(shard_piece.shape), "row", scatter_dimension=1, tiled=True
    )
    returned = lax.all_to_all(summed, VOCAB_AXES, split_axis=1, concat_axis=1, tiled=True)
    combine = selector * weights.T[:, None, :]
    moe_sum = jnp.einsum(
        "esr,sed->rd", combine, returned.astype(jnp.float32), precision=lax.Precision.HIGHEST
    )
    mixed_rows = resid_in + moe_sum
    final_normed = rms_norm(mixed_rows, head_gain).astype(jnp.bfloat16)
    gathered = lax.all_gather(final_normed, ALL_AXES, axis=0, tiled=False)
    logits = jnp.einsum("gtd,wd->gtw", gathered, head, preferred_element_type=jnp.float32)
    target_logits = logits.reshape(requests, slot_total, local_vocab)
    pick_target = jnp.sum(jnp.where(id_match, target_logits[:, :DRAFTS], 0.0), axis=-1)
    top_target = tree_pmax(jnp.max(target_logits, axis=-1))
    target_exp = jnp.exp(target_logits - top_target[:, :, None])
    sum_target, pick_t = tree_psum((jnp.sum(target_exp, axis=-1), pick_target))
    target = target_exp / sum_target[:, :, None]
    draft_prob = draft_exp / sum_draft[:, :, None]
    log_target = pick_t - top_target[:, :DRAFTS] - jnp.log(sum_target[:, :DRAFTS])
    log_draft = pick_d - top_draft - jnp.log(sum_draft)
    accept = jnp.exp(jnp.minimum(log_target - log_draft, 0.0))
    position = (jnp.arange(slot_total, dtype=jnp.int32)[None, :] == reject_pos[:, None]).astype(
        jnp.float32
    )
    target_at = jnp.sum(position[:, :, None] * target, axis=1)
    draft_at = jnp.sum(position[:, :DRAFTS, None] * draft_prob, axis=1)
    gap_rows = jnp.maximum(target_at - draft_at, 0.0)
    gap_total = tree_psum(jnp.sum(gap_rows, axis=-1))
    residual = jnp.sqrt(V * gap_rows / gap_total[:, None])
    return (residual, accept)


def solution(mesh):
    row_size, vocab_size = mesh.devices.shape
    split = (row_size, 4, vocab_size // 8, 2)
    fine = Mesh(np.asarray(mesh.devices).reshape(split), ALL_AXES)
    spread = ALL_AXES
    placed = (
        P(spread, None),
        P(),
        P(),
        P(spread, None),
        P(VOCAB_AXES, None, "row"),
        P(VOCAB_AXES, None, "row"),
        P(VOCAB_AXES, "row", None),
        P(),
        P(spread, None),
        P(None, None, spread),
        P(),
        P(),
    )
    return jax.shard_map(
        body, mesh=fine, in_specs=placed, out_specs=(P(None, spread), P()), check_vma=False
    )
```

profile of v0, /device:TPU:0, one launch (start us, length us, event | category | flops | bytes accessed | tf_op | source)
XLA Modules:
  0.0 651.1 jit_solution(5099887849405684737)
XLA Ops:
  9.3 1.5 fusion.2
  12.0 33.8 %all_to_all.10 = bf16[3,32,7168]{2,0,1:T(4,128)(2,1)S(1)} all-to-all(bf16[3,32,7168]{2,0,1:T(4,128)(2,1)S(1)} %copy.63), channel_id=1, replica_groups=mesh['row'=4,'vz'=4,'vx'=4,'core'=2] {'vz','vx','core'}, dimensions={1} | all-to-all | bytes 2752512 | tf_op jit(solution)/shard_map/all_to_all | solution.py:83
  45.9 1.7 copy.64
  48.0 56.5 %all-gather.5.cloned.1.call-done = bf16[3,128,7168]{2,1,0:T(8,128)(2,1)} async-done(((bf16[3,32,7168]{2,1,0:T(8,128)(2,1)}), bf16[3,128,7168]{2,1,0:T(8,128)(2,1)}) %all-gather.5.cloned.1.call-update) | async-done | bytes 5505040 | tf_op jit(solution)/shard_map/all_gather | solution.py:84
  104.6 5.4 fusion.8
  110.9 1.6 fusion.21
  113.0 4.0 convolution_convert_fusion
  117.0 10.3 %copy.65 = bf16[3,128,7168]{2,0,1:T(4,128)(2,1)} copy(bf16[3,128,7168]{2,1,0:T(8,128)(2,1)} %bitcast.48) | data formatting | bytes 11010048 | tf_op jit(solution)/shard_map/reshape | solution.py:91
  129.2 142.7 %all-reduce.15.cloned.1.call-done = bf16[3,128,7168]{2,0,1:T(4,128)(2,1)} async-done(((bf16[3,128,7168]{2,0,1:T(4,128)(2,1)}), bf16[3,128,7168]{2,0,1:T(4,128)(2,1)}) %all-reduce.15.cloned.1.call-update) | async-done | bytes 5505040
  271.9 3.5 constant_dynamic-slice_fusion
  275.3 7.4 %all-to-all-start.1 = ((bf16[3,32,7168]{2,0,1:T(4,128)(2,1)}), bf16[3,32,7168]{2,0,1:T(4,128)(2,1)S(1)}, u32[]{:S(2)}, u32[]{:S(2)}) async-start(bf16[3,32,7168]{2,0,1:T(4,128)(2,1)} %constant_dynamic-slice_fusion), calls=%async_computation.1 | async-start | bytes 3670016 | tf_op jit(solution)/shard_map/all_to_all | solution.py:93
  284.2 25.5 %all-to-all-done.1 = bf16[3,32,7168]{2,0,1:T(4,128)(2,1)S(1)} async-done(((bf16[3,32,7168]{2,0,1:T(4,128)(2,1)}), bf16[3,32,7168]{2,0,1:T(4,128)(2,1)S(1)}, u32[]{:S(2)}, u32[]{:S(2)}) %all-to-all-start.1) | async-done | bytes 1376288 | tf_op jit(solution)/shard_map/all_to_all | solution.py:93
  309.7 2.3 multiply_reduce_fusion.1
  314.4 94.2 %all-gather.7.cloned.1.call-done = bf16[128,10,7168]{2,1,0:T(8,128)(2,1)} async-done(((bf16[1,10,7168]{2,1,0:T(8,128)(2,1)}), bf16[128,10,7168]{2,1,0:T(8,128)(2,1)}) %all-gather.7.cloned.1.call-update) | async-done | bytes 18350096 | tf_op jit(solution)/shard_map/all_gather | solution.py:100
  408.6 32.2 %fusion.53 = (f32[128,10]{0,1:T(8,128)S(1)}, f32[128,10,512]{2,0,1:T(8,128)S(1)}) fusion(bf16[512,7168]{1,0:T(8,128)(2,1)} %param.20, bf16[128,10,7168]{2,1,0:T(8,128)(2,1)} %all-gather.7.cloned.1.call-done), kind=kOutput, calls=%fused_computation.75 | convolution fusion | flops 9395895296 | bytes 28316672 | tf_op jit(solution)/shard_map/gtd,wd->gtw/dot_general | solution.py:101
  441.0 4.2 all-reduce.12
  445.2 20.1 %all-reduce.7 = (f32[256,5]{1,0:T(8,128)S(1)}, f32[256,4]{1,0:T(8,128)S(1)}) all-reduce(f32[256,5]{1,0:T(8,128)S(1)} %get-tuple-element.41, f32[256,4]{1,0:T(8,128)S(1)} %get-tuple-element.42), channel_id=1, replica_groups=mesh['row'=4,'vz'=4,'vx'=4,'core'=2] {'vx'}, use_global_device_ids=true, to_apply=%region_8.9 | all-reduce | flops 2304 | bytes 18432 | tf_op jit(solution)/shard_map/pmax | solution.py:27
  465.4 18.6 %all-reduce.8 = (f32[256,5]{1,0:T(8,128)S(1)}, f32[256,4]{1,0:T(8,128)S(1)}) all-reduce(f32[256,5]{1,0:T(8,128)S(1)} %get-tuple-element.30, f32[256,4]{1,0:T(8,128)S(1)} %get-tuple-element.31), channel_id=1, replica_groups=mesh['row'=4,'vz'=4,'vx'=4,'core'=2] {'vz'}, use_global_device_ids=true, to_apply=%region_9.10 | all-reduce | flops 2304 | bytes 18432 | tf_op jit(solution)/shard_map/pmax | solution.py:27
  484.0 19.0 %all-reduce.9 = (f32[256,5]{1,0:T(8,128)S(1)}, f32[256,4]{1,0:T(8,128)S(1)}) all-reduce(f32[256,5]{1,0:T(8,128)S(1)} %get-tuple-element.32, f32[256,4]{1,0:T(8,128)S(1)} %get-tuple-element.33), channel_id=1, replica_groups=mesh['row'=4,'vz'=4,'vx'=4,'core'=2] {'row'}, use_global_device_ids=true, to_apply=%region_10.11 | all-reduce | flops 2304 | bytes 18432 | tf_op jit(solution)/shard_map/pmax | solution.py:27
  503.2 3.6 copy.68
  507.7 2.3 fusion.12
  510.0 4.8 reshape.70
  514.8 4.1 all-reduce.11
  518.9 18.1 %all-reduce.2 = (f32[256,5]{1,0:T(8,128)S(1)}, f32[256,4]{1,0:T(8,128)S(1)}) all-reduce(f32[256,5]{1,0:T(8,128)S(1)} %get-tuple-element.39, f32[256,4]{1,0:T(8,128)S(1)} %get-tuple-element.40), channel_id=1, replica_groups=mesh['row'=4,'vz'=4,'vx'=4,'core'=2] {'vx'}, use_global_device_ids=true, to_apply=%region_13.14 | all-reduce | flops 2304 | bytes 18432 | tf_op jit(solution)/shard_map/psum | solution.py:21
  537.0 17.8 %all-reduce.4 = (f32[256,5]{1,0:T(8,128)S(1)}, f32[256,4]{1,0:T(8,128)S(1)}) all-reduce(f32[256,5]{1,0:T(8,128)S(1)} %get-tuple-element.18, f32[256,4]{1,0:T(8,128)S(1)} %get-tuple-element.19), channel_id=1, replica_groups=mesh['row'=4,'vz'=4,'vx'=4,'core'=2] {'vz'}, use_global_device_ids=true, to_apply=%region_14.15 | all-reduce | flops 2304 | bytes 18432 | tf_op jit(solution)/shard_map/psum | solution.py:21
  554.8 17.0 %all-reduce.6 = (f32[256,5]{1,0:T(8,128)S(1)}, f32[256,4]{1,0:T(8,128)S(1)}) all-reduce(f32[256,5]{1,0:T(8,128)S(1)} %get-tuple-element.23, f32[256,4]{1,0:T(8,128)S(1)} %get-tuple-element.24), channel_id=1, replica_groups=mesh['row'=4,'vz'=4,'vx'=4,'core'=2] {'row'}, use_global_device_ids=true, to_apply=%region_15.16 | all-reduce | flops 2304 | bytes 18432 | tf_op jit(solution)/shard_map/psum | solution.py:21
  571.9 3.8 multiply_reduce_fusion
  575.8 5.6 fusion.14
  581.5 4.7 all-reduce.10
  586.2 20.3 %all-reduce.1 = (f32[256]{0:T(256)S(1)}, f32[256,4]{1,0:T(8,128)S(1)}, f32[256,4]{1,0:T(8,128)S(1)}) all-reduce(f32[256]{0:T(256)S(1)} %get-tuple-element.36, f32[256,4]{1,0:T(8,128)S(1)} %get-tuple-element.37, f32[256,4]{1,0:T(8,128)S(1)} %get-tuple-element.38), channel_id=1, replica_groups=mesh['row'=4,'vz'=4,'vx'=4,'core'=2] {'vx'}, use_global_device_ids=true, to_apply=%region_30.31 | all-reduce | flops 2304 | bytes 18432 | tf_op jit(solution)/shard_map/psum | solution.py:21
  606.5 17.1 %all-reduce.3 = (f32[256]{0:T(256)S(1)}, f32[256,4]{1,0:T(8,128)S(1)}, f32[256,4]{1,0:T(8,128)S(1)}) all-reduce(f32[256]{0:T(256)S(1)} %get-tuple-element.15, f32[256,4]{1,0:T(8,128)S(1)} %get-tuple-element.16, f32[256,4]{1,0:T(8,128)S(1)} %get-tuple-element.17), channel_id=1, replica_groups=mesh['row'=4,'vz'=4,'vx'=4,'core'=2] {'vz'}, use_global_device_ids=true, to_apply=%region_31.32 | all-reduce | flops 2304 | bytes 18432 | tf_op jit(solution)/shard_map/psum | solution.py:21
  623.6 18.9 %all-reduce.5 = (f32[256]{0:T(256)S(1)}, f32[256,4]{1,0:T(8,128)S(1)}, f32[256,4]{1,0:T(8,128)S(1)}) all-reduce(f32[256]{0:T(256)S(1)} %get-tuple-element.20, f32[256,4]{1,0:T(8,128)S(1)} %get-tuple-element.21, f32[256,4]{1,0:T(8,128)S(1)} %get-tuple-element.22), channel_id=1, replica_groups=mesh['row'=4,'vz'=4,'vx'=4,'core'=2] {'row'}, use_global_device_ids=true, to_apply=%region_32.33 | all-reduce | flops 2304 | bytes 18432 | tf_op jit(solution)/shard_map/psum | solution.py:21
  (62 shorter events, 13.4 us)
Async XLA Ops:
  7.2 275.6 %copy-start = (bf16[7168,32]{0,1:T(8,128)(2,1)S(1)}, bf16[7168,32]{0,1:T(8,128)(2,1)}, u32[]{:S(2)}) copy-start(bf16[7168,32]{0,1:T(8,128)(2,1)} %param.14) | copy-start | bytes 1376260
  7.2 97.4 %all-gather.5.cloned.1.call-start = ((), (), s32[]{:S(2)}) async-start(), calls=%async_computation.2 | async-start | bytes 6881280 | tf_op jit(solution)/shard_map/all_gather | solution.py:84
  47.5 224.3 %all-reduce.15.cloned.1.call-start = ((), (), s32[]{:S(2)}) async-start(), calls=%async_computation.4 | async-start | bytes 14680064
  104.6 5.4 copy-start.11
  104.6 6.3 copy-start.12
  110.9 2.0 copy-start.5
  127.3 0.7 copy-start.13
  129.2 153.6 %copy-start.7 = (f32[7168]{0:T(1024)S(1)}, f32[7168]{0:T(1024)}, u32[]{:S(2)}) copy-start(f32[7168]{0:T(1024)} %param.13) | copy-start | bytes 86020
  275.3 36.7 %copy-start.8 = (f32[7168]{0:T(1024)S(1)}, f32[7168]{0:T(1024)}, u32[]{:S(2)}) copy-start(f32[7168]{0:T(1024)} %param.19) | copy-start | bytes 86020
  275.3 37.6 %copy-start.9 = (s32[256,4]{0,1:T(4,128)S(1)}, s32[256,4]{0,1:T(4,128)}, u32[]{:S(2)}) copy-start(s32[256,4]{0,1:T(4,128)} %param.22) | copy-start | bytes 12292
  275.3 38.4 %copy-start.3 = (bf16[256,4,512]{2,1,0:T(4,128)(2,1)S(1)}, bf16[256,4,512]{2,1,0:T(4,128)(2,1)}, u32[]{:S(2)}) copy-start(bf16[256,4,512]{2,1,0:T(4,128)(2,1)} %param.21) | copy-start | bytes 3145732
  275.3 38.9 %copy-start.10 = (s32[256]{0:T(256)S(1)}, s32[256]{0:T(256)}, u32[]{:S(2)}) copy-start(s32[256]{0:T(256)} %param.23) | copy-start | bytes 3076
  275.3 34.4 %all-to-all-start.1 = ((bf16[3,32,7168]{2,0,1:T(4,128)(2,1)}), bf16[3,32,7168]{2,0,1:T(4,128)(2,1)S(1)}, u32[]{:S(2)}, u32[]{:S(2)}) async-start(bf16[3,32,7168]{2,0,1:T(4,128)(2,1)} %constant_dynamic-slice_fusion), calls=%async_computation.1 | async-start | bytes 3670016 | tf_op jit(solution)/shard_map/all_to_all | solution.py:93
  282.7 125.9 %all-gather.7.cloned.1.call-start = ((), (), s32[]{:S(2)}) async-start(), calls=%async_computation.3 | async-start | bytes 29589504 | tf_op jit(solution)/shard_map/all_gather | solution.py:100
  514.7 61.0 %copy-start.4 = (bf16[256,4,512]{2,1,0:T(4,128)(2,1)S(1)}, bf16[256,4,512]{2,1,0:T(4,128)(2,1)}, u32[]{:S(2)}) copy-start(bf16[256,4,512]{2,1,0:T(4,128)(2,1)} %param.21) | copy-start | bytes 3145732
  514.7 61.0 %copy-start.6 = (s32[256,4]{1,0:T(8,128)S(1)}, s32[256,4]{1,0:T(8,128)}, u32[]{:S(2)}) copy-start(s32[256,4]{1,0:T(8,128)} %copy.72) | copy-start | bytes 12292
  571.8 3.9 copy-start.2
  575.7 68.6 %copy-start.1 = (bf16[7168,32]{0,1:T(8,128)(2,1)S(1)}, bf16[7168,32]{0,1:T(8,128)(2,1)}, u32[]{:S(2)}) copy-start(bf16[7168,32]{0,1:T(8,128)(2,1)} %param.14) | copy-start | bytes 1376260
Sparse Core Ops, SparseCore 0:
  47.7 56.8 all-gather.4
  127.4 144.4 all-reduce.14
  313.0 95.5 all-gather.6
where the time goes:
time: 655 us; the launch traced here: 651 us
  waiting for transfers between devices  319 us (49%)
  blocking collectives  214 us (33%)
  matrix products  48.4 us (7%)
  local copies, waits for them, and re-layouts  30.4 us (5%)
  other arithmetic  16.4 us (3%)
  between operations  15 us (2%)
  starting transfers between devices  7.96 us (1%)
    unnamed x4, waiting for transfers between devices  143 us
    psum x8, blocking collectives, tree_psum(): values = lax.psum(values, axis)  118 us
    all_gather x1, waiting for transfers between devices, body(): gathered = lax.all_gather(final_normed, ALL_AXES, axis=0, tiled=False)  94.2 us
    pmax x4, blocking collectives, tree_pmax(): values = lax.pmax(values, axis)  62 us
    all_gather x1, waiting for transfers between devices, body(): shard_piece = lax.all_gather(received, 'row', axis=1, tiled=True)  56.5 us
    all_to_all x1, blocking collectives, body(): lax.all_to_all(send_buffer, VOCAB_AXES, split_axis=1, concat_axis=1, tile...  33.8 us
    dot_general x1, matrix products, body(): jnp.einsum('gtd,wd->gtw', gathered, head, preferred_element_type=jnp.floa...  32.2 us
    all_to_all x1, waiting for transfers between devices, body(): lax.all_to_all(summed, VOCAB_AXES, split_axis=1, concat_axis=1, tiled=True)  25.5 us
  transfers between devices with their start and end apart: 4, of which 4 were waited for; matrix products, arithmetic and copies ran while one was open for 1% of the time, Pallas kernels for 0%

commit v1 on v0

--- a/solution.py
+++ b/solution.py
@@ -81,7 +81,24 @@
     up_w = w_up[0]
     down_w = w_down[0]
     received = lax.all_to_all(send_buffer, VOCAB_AXES, split_axis=1, concat_axis=1, tiled=True)
-    shard_piece = lax.all_gather(received, "row", axis=1, tiled=True)
+    size, index, rows = (lax.axis_size("row"), lax.axis_index("row"), received.shape[1])
+    right = [(i, (i + 1) % size) for i in range(size)]
+    behind = [(i, (i - 1) % size) for i in range(size)]
+    result = jnp.zeros((*received.shape[:1], size * rows, *received.shape[1 + 1 :]), received.dtype)
+    result = lax.dynamic_update_slice_in_dim(result, received, index * rows, axis=1)
+    from_left = from_right = received
+    half = size // 2
+    for step in range(1, half + 1):
+        from_left = lax.ppermute(from_left, "row", right)
+        result = lax.dynamic_update_slice_in_dim(
+            result, from_left, (index - step) % size * rows, axis=1
+        )
+        if step < size - half:
+            from_right = lax.ppermute(from_right, "row", behind)
+            result = lax.dynamic_update_slice_in_dim(
+                result, from_right, (index + step) % size * rows, axis=1
+            )
+    shard_piece = result
     flat_rows = shard_piece.reshape(-1, model_width)
     gate_out = jnp.dot(flat_rows, gate_w, preferred_element_type=jnp.float32)
     up_out = jnp.dot(flat_rows, up_w, preferred_element_type=jnp.float32)

time: 655 us -> 667 us (1.018)
  blocking collectives: 214 us -> 180 us
  waiting for transfers between devices: 319 us -> 345 us
  starting transfers between devices: 7.96 us -> 19.7 us
  local copies, waits for them, and re-layouts: 30.4 us -> 38.3 us
    ppermute x0 -> x3, waiting for transfers between devices: none -> 58.3 us  [the longest x2 58.3 us: body(): from_left = lax.ppermute(from_left, 'row', right)]
    all_gather x1 -> x0, waiting for transfers between devices: 56.5 us -> none  [body(): shard_piece = lax.all_gather(received, 'row', axis=1, tiled=True)]
    all_to_all x1 -> x0, blocking collectives: 33.8 us -> none  [body(): lax.all_to_all(send_buffer, VOCAB_AXES, split_axis=1, concat_axis=1, tile...]
    all_to_all x0 -> x1, waiting for transfers between devices: none -> 27 us  [body(): lax.all_to_all(send_buffer, VOCAB_AXES, split_axis=1, concat_axis=1, tile...]
    all_to_all x0 -> x1, starting transfers between devices: none -> 8.28 us  [body(): lax.all_to_all(send_buffer, VOCAB_AXES, split_axis=1, concat_axis=1, tile...]
    unnamed x4 -> x3, waiting for transfers between devices: 143 us -> 140 us
  transfers between devices with their start and end apart: 4 -> 7, of which waited for: 4 -> 6; matrix products, arithmetic and copies ran while one was open for 1% -> 1% of each run, Pallas kernels for 0% -> 0%
where the time goes in v1:
time: 667 us; the launch traced here: 662 us
  waiting for transfers between devices  345 us (52%)
  blocking collectives  180 us (27%)
  matrix products  47.4 us (7%)
  local copies, waits for them, and re-layouts  38.3 us (6%)
  starting transfers between devices  19.7 us (3%)
  other arithmetic  16.5 us (2%)
  between operations  15.3 us (2%)
    unnamed x3, waiting for transfers between devices  140 us
    psum x8, blocking collectives, tree_psum(): values = lax.psum(values, axis)  118 us
    all_gather x1, waiting for transfers between devices, body(): gathered = lax.all_gather(final_normed, ALL_AXES, axis=0, tiled=False)  94.2 us
    pmax x4, blocking collectives, tree_pmax(): values = lax.pmax(values, axis)  62 us
    ppermute x2, waiting for transfers between devices, body(): from_left = lax.ppermute(from_left, 'row', right)  58.3 us
    dot_general x1, matrix products, body(): jnp.einsum('gtd,wd->gtw', gathered, head, preferred_element_type=jnp.floa...  32.2 us
    all_to_all x1, waiting for transfers between devices, body(): lax.all_to_all(send_buffer, VOCAB_AXES, split_axis=1, concat_axis=1, tile...  27 us
    all_to_all x1, waiting for transfers between devices, body(): lax.all_to_all(summed, VOCAB_AXES, split_axis=1, concat_axis=1, tiled=True)  25.5 us
  transfers between devices with their start and end apart: 7, of which 6 were waited for; matrix products, arithmetic and copies ran while one was open for 1% of the time, Pallas kernels for 0%

profile of v1, /device:TPU:0, one launch (start us, length us, event | category | flops | bytes accessed | tf_op | source)
XLA Modules:
  0.0 662.2 jit_solution(7420648498835805055)
XLA Ops:
  10.8 2.4 copy.67
  13.2 8.3 %all-to-all-start = ((bf16[3,32,7168]{2,0,1:T(4,128)(2,1)}), bf16[3,32,7168]{2,0,1:T(4,128)(2,1)S(1)}, u32[]{:S(2)}, u32[]{:S(2)}) async-start(bf16[3,32,7168]{2,0,1:T(4,128)(2,1)} %copy.67), calls=%async_computation | async-start | bytes 3670016 | tf_op jit(solution)/shard_map/all_to_all | solution.py:83
  21.6 27.0 %all-to-all-done = bf16[3,32,7168]{2,0,1:T(4,128)(2,1)S(1)} async-done(((bf16[3,32,7168]{2,0,1:T(4,128)(2,1)}), bf16[3,32,7168]{2,0,1:T(4,128)(2,1)S(1)}, u32[]{:S(2)}, u32[]{:S(2)}) %all-to-all-start) | async-done | bytes 1376288 | tf_op jit(solution)/shard_map/all_to_all | solution.py:83
  50.9 2.4 copy-done.5
  56.5 29.4 %collective-permute-done = bf16[3,32,7168]{2,1,0:T(8,128)(2,1)S(1)} collective-permute-done((bf16[3,32,7168]{2,1,0:T(8,128)(2,1)}, bf16[3,32,7168]{2,1,0:T(8,128)(2,1)S(1)}, u32[]{:S(2)}, u32[]{:S(2)}) %collective-permute-start) | collective-permute-done | bytes 1376288 | tf_op jit(solution)/shard_map/ppermute | solution.py:92
  89.1 28.9 %collective-permute-done.2 = bf16[3,32,7168]{2,1,0:T(8,128)(2,1)S(1)} collective-permute-done((bf16[3,32,7168]{2,1,0:T(8,128)(2,1)S(1)}, bf16[3,32,7168]{2,1,0:T(8,128)(2,1)S(1)}, u32[]{:S(2)}, u32[]{:S(2)}) %collective-permute-start.2) | collective-permute-done | bytes 1376288 | tf_op jit(solution)/shard_map/ppermute | solution.py:92
  119.2 4.3 fusion.6
  126.5 4.0 convolution_convert_fusion
  130.5 10.3 %copy.71 = bf16[3,128,7168]{2,0,1:T(4,128)(2,1)} copy(bf16[3,128,7168]{2,1,0:T(8,128)(2,1)} %bitcast.43) | data formatting | bytes 11010048 | tf_op jit(solution)/shard_map/reshape | solution.py:108
  142.7 139.9 %all-reduce.15.cloned.1.call-done = bf16[3,128,7168]{2,0,1:T(4,128)(2,1)} async-done(((bf16[3,128,7168]{2,0,1:T(4,128)(2,1)}), bf16[3,128,7168]{2,0,1:T(4,128)(2,1)}) %all-reduce.15.cloned.1.call-update) | async-done | bytes 5505040
  282.6 3.5 constant_dynamic-slice_fusion
  286.1 7.4 %all-to-all-start.1 = ((bf16[3,32,7168]{2,0,1:T(4,128)(2,1)}), bf16[3,32,7168]{2,0,1:T(4,128)(2,1)S(1)}, u32[]{:S(2)}, u32[]{:S(2)}) async-start(bf16[3,32,7168]{2,0,1:T(4,128)(2,1)} %constant_dynamic-slice_fusion), calls=%async_computation.1 | async-start | bytes 3670016 | tf_op jit(solution)/shard_map/all_to_all | solution.py:110
  295.0 25.5 %all-to-all-done.1 = bf16[3,32,7168]{2,0,1:T(4,128)(2,1)S(1)} async-done(((bf16[3,32,7168]{2,0,1:T(4,128)(2,1)}), bf16[3,32,7168]{2,0,1:T(4,128)(2,1)S(1)}, u32[]{:S(2)}, u32[]{:S(2)}) %all-to-all-start.1) | async-done | bytes 1376288 | tf_op jit(solution)/shard_map/all_to_all | solution.py:110
  320.5 2.3 multiply_reduce_fusion.1
  325.1 94.2 %all-gather.4.cloned.1.call-done = bf16[128,10,7168]{2,1,0:T(8,128)(2,1)} async-done(((bf16[1,10,7168]{2,1,0:T(8,128)(2,1)}), bf16[128,10,7168]{2,1,0:T(8,128)(2,1)}) %all-gather.4.cloned.1.call-update) | async-done | bytes 18350096 | tf_op jit(solution)/shard_map/all_gather | solution.py:117
  419.4 32.2 %fusion.49 = (f32[128,10]{0,1:T(8,128)S(1)}, f32[128,10,512]{2,0,1:T(8,128)S(1)}) fusion(bf16[512,7168]{1,0:T(8,128)(2,1)} %param.20, bf16[128,10,7168]{2,1,0:T(8,128)(2,1)} %all-gather.4.cloned.1.call-done), kind=kOutput, calls=%fused_computation.80 | convolution fusion | flops 9395895296 | bytes 28316672 | tf_op jit(solution)/shard_map/gtd,wd->gtw/dot_general | solution.py:118
  451.8 4.2 all-reduce.12
  456.0 20.1 %all-reduce.7 = (f32[256,5]{1,0:T(8,128)S(1)}, f32[256,4]{1,0:T(8,128)S(1)}) all-reduce(f32[256,5]{1,0:T(8,128)S(1)} %get-tuple-element.41, f32[256,4]{1,0:T(8,128)S(1)} %get-tuple-element.42), channel_id=1, replica_groups=mesh['row'=4,'vz'=4,'vx'=4,'core'=2] {'vx'}, use_global_device_ids=true, to_apply=%region_8.9 | all-reduce | flops 2304 | bytes 18432 | tf_op jit(solution)/shard_map/pmax | solution.py:27
  476.2 18.6 %all-reduce.8 = (f32[256,5]{1,0:T(8,128)S(1)}, f32[256,4]{1,0:T(8,128)S(1)}) all-reduce(f32[256,5]{1,0:T(8,128)S(1)} %get-tuple-element.30, f32[256,4]{1,0:T(8,128)S(1)} %get-tuple-element.31), channel_id=1, replica_groups=mesh['row'=4,'vz'=4,'vx'=4,'core'=2] {'vz'}, use_global_device_ids=true, to_apply=%region_9.10 | all-reduce | flops 2304 | bytes 18432 | tf_op jit(solution)/shard_map/pmax | solution.py:27
  494.8 19.0 %all-reduce.9 = (f32[256,5]{1,0:T(8,128)S(1)}, f32[256,4]{1,0:T(8,128)S(1)}) all-reduce(f32[256,5]{1,0:T(8,128)S(1)} %get-tuple-element.32, f32[256,4]{1,0:T(8,128)S(1)} %get-tuple-element.33), channel_id=1, replica_groups=mesh['row'=4,'vz'=4,'vx'=4,'core'=2] {'row'}, use_global_device_ids=true, to_apply=%region_10.11 | all-reduce | flops 2304 | bytes 18432 | tf_op jit(solution)/shard_map/pmax | solution.py:27
  514.0 3.6 copy.74
  520.8 4.8 reshape.70
  525.5 4.1 all-reduce.11
  529.7 18.1 %all-reduce.2 = (f32[256,5]{1,0:T(8,128)S(1)}, f32[256,4]{1,0:T(8,128)S(1)}) all-reduce(f32[256,5]{1,0:T(8,128)S(1)} %get-tuple-element.39, f32[256,4]{1,0:T(8,128)S(1)} %get-tuple-element.40), channel_id=1, replica_groups=mesh['row'=4,'vz'=4,'vx'=4,'core'=2] {'vx'}, use_global_device_ids=true, to_apply=%region_13.14 | all-reduce | flops 2304 | bytes 18432 | tf_op jit(solution)/shard_map/psum | solution.py:21
  547.8 17.8 %all-reduce.4 = (f32[256,5]{1,0:T(8,128)S(1)}, f32[256,4]{1,0:T(8,128)S(1)}) all-reduce(f32[256,5]{1,0:T(8,128)S(1)} %get-tuple-element.18, f32[256,4]{1,0:T(8,128)S(1)} %get-tuple-element.19), channel_id=1, replica_groups=mesh['row'=4,'vz'=4,'vx'=4,'core'=2] {'vz'}, use_global_device_ids=true, to_apply=%region_14.15 | all-reduce | flops 2304 | bytes 18432 | tf_op jit(solution)/shard_map/psum | solution.py:21
  565.6 17.0 %all-reduce.6 = (f32[256,5]{1,0:T(8,128)S(1)}, f32[256,4]{1,0:T(8,128)S(1)}) all-reduce(f32[256,5]{1,0:T(8,128)S(1)} %get-tuple-element.23, f32[256,4]{1,0:T(8,128)S(1)} %get-tuple-element.24), channel_id=1, replica_groups=mesh['row'=4,'vz'=4,'vx'=4,'core'=2] {'row'}, use_global_device_ids=true, to_apply=%region_15.16 | all-reduce | flops 2304 | bytes 18432 | tf_op jit(solution)/shard_map/psum | solution.py:21
  582.6 3.8 multiply_reduce_fusion
  586.5 5.6 fusion.14
  592.3 4.7 all-reduce.10
  597.0 20.3 %all-reduce.1 = (f32[256]{0:T(256)S(1)}, f32[256,4]{1,0:T(8,128)S(1)}, f32[256,4]{1,0:T(8,128)S(1)}) all-reduce(f32[256]{0:T(256)S(1)} %get-tuple-element.36, f32[256,4]{1,0:T(8,128)S(1)} %get-tuple-element.37, f32[256,4]{1,0:T(8,128)S(1)} %get-tuple-element.38), channel_id=1, replica_groups=mesh['row'=4,'vz'=4,'vx'=4,'core'=2] {'vx'}, use_global_device_ids=true, to_apply=%region_30.31 | all-reduce | flops 2304 | bytes 18432 | tf_op jit(solution)/shard_map/psum | solution.py:21
  617.3 17.1 %all-reduce.3 = (f32[256]{0:T(256)S(1)}, f32[256,4]{1,0:T(8,128)S(1)}, f32[256,4]{1,0:T(8,128)S(1)}) all-reduce(f32[256]{0:T(256)S(1)} %get-tuple-element.15, f32[256,4]{1,0:T(8,128)S(1)} %get-tuple-element.16, f32[256,4]{1,0:T(8,128)S(1)} %get-tuple-element.17), channel_id=1, replica_groups=mesh['row'=4,'vz'=4,'vx'=4,'core'=2] {'vz'}, use_global_device_ids=true, to_apply=%region_31.32 | all-reduce | flops 2304 | bytes 18432 | tf_op jit(solution)/shard_map/psum | solution.py:21
  634.4 18.9 %all-reduce.5 = (f32[256]{0:T(256)S(1)}, f32[256,4]{1,0:T(8,128)S(1)}, f32[256,4]{1,0:T(8,128)S(1)}) all-reduce(f32[256]{0:T(256)S(1)} %get-tuple-element.20, f32[256,4]{1,0:T(8,128)S(1)} %get-tuple-element.21, f32[256,4]{1,0:T(8,128)S(1)} %get-tuple-element.22), channel_id=1, replica_groups=mesh['row'=4,'vz'=4,'vx'=4,'core'=2] {'row'}, use_global_device_ids=true, to_apply=%region_32.33 | all-reduce | flops 2304 | bytes 18432 | tf_op jit(solution)/shard_map/psum | solution.py:21
  (74 shorter events, 27.0 us)
Async XLA Ops:
  7.2 286.4 %copy-start = (bf16[7168,32]{0,1:T(8,128)(2,1)S(1)}, bf16[7168,32]{0,1:T(8,128)(2,1)}, u32[]{:S(2)}) copy-start(bf16[7168,32]{0,1:T(8,128)(2,1)} %param.14) | copy-start | bytes 1376260
  13.2 35.3 %all-to-all-start = ((bf16[3,32,7168]{2,0,1:T(4,128)(2,1)}), bf16[3,32,7168]{2,0,1:T(4,128)(2,1)S(1)}, u32[]{:S(2)}, u32[]{:S(2)}) async-start(bf16[3,32,7168]{2,0,1:T(4,128)(2,1)} %copy.67), calls=%async_computation | async-start | bytes 3670016 | tf_op jit(solution)/shard_map/all_to_all | solution.py:83
  21.5 261.1 %all-reduce.15.cloned.1.call-start = ((), (), s32[]{:S(2)}) async-start(), calls=%async_computation.3 | async-start | bytes 14680064
  50.9 2.4 copy-start.5
  53.3 32.6 %collective-permute-start = (bf16[3,32,7168]{2,1,0:T(8,128)(2,1)}, bf16[3,32,7168]{2,1,0:T(8,128)(2,1)S(1)}, u32[]{:S(2)}, u32[]{:S(2)}) collective-permute-start(bf16[3,32,7168]{2,1,0:T(8,128)(2,1)} %get-tuple-element.44), channel_id=1, source_target_pairs={{0,32},{32,64},{64,96},{96,0},{1,33},{33,65},{65,97},{97,1},{2,34}... | collective-permute-start | bytes 4128776 | tf_op jit(solution)/shard_map/ppermute | solution.py:92
  54.9 33.0 %collective-permute-start.1 = (bf16[3,32,7168]{2,1,0:T(8,128)(2,1)}, bf16[3,32,7168]{2,1,0:T(8,128)(2,1)S(1)}, u32[]{:S(2)}, u32[]{:S(2)}) collective-permute-start(bf16[3,32,7168]{2,1,0:T(8,128)(2,1)} %get-tuple-element.44), channel_id=1, source_target_pairs={{0,96},{32,0},{64,32},{96,64},{1,97},{33,1},{65,33},{97,65},{2,98}... | collective-permute-start | bytes 4128776 | tf_op jit(solution)/shard_map/ppermute | solution.py:97
  86.0 32.0 %collective-permute-start.2 = (bf16[3,32,7168]{2,1,0:T(8,128)(2,1)S(1)}, bf16[3,32,7168]{2,1,0:T(8,128)(2,1)S(1)}, u32[]{:S(2)}, u32[]{:S(2)}) collective-permute-start(bf16[3,32,7168]{2,1,0:T(8,128)(2,1)S(1)} %collective-permute-done), channel_id=1, source_target_pairs={{0,32},{32,64},{64,96},{96,0},{1,33},{33,65},{65,97},{97,1},{2,34}... | collective-permute-start | bytes 4128776 | tf_op jit(solution)/shard_map/ppermute | solution.py:92
  86.7 32.5 %copy-start.13 = (bf16[1,7168,256]{2,1,0:T(8,128)(2,1)S(1)}, bf16[1,7168,256]{2,1,0:T(8,128)(2,1)}, u32[]{:S(2)}) copy-start(bf16[1,7168,256]{2,1,0:T(8,128)(2,1)} %param.17) | copy-start | bytes 11010052
  119.2 4.4 copy-start.6
  119.2 5.3 copy-start.14
  124.5 2.0 copy-start.7
  140.8 0.7 copy-start.15
  142.7 150.9 %copy-start.9 = (f32[7168]{0:T(1024)S(1)}, f32[7168]{0:T(1024)}, u32[]{:S(2)}) copy-start(f32[7168]{0:T(1024)} %param.13) | copy-start | bytes 86020
  286.1 36.7 %copy-start.10 = (f32[7168]{0:T(1024)S(1)}, f32[7168]{0:T(1024)}, u32[]{:S(2)}) copy-start(f32[7168]{0:T(1024)} %param.19) | copy-start | bytes 86020
  286.1 37.6 %copy-start.11 = (s32[256,4]{0,1:T(4,128)S(1)}, s32[256,4]{0,1:T(4,128)}, u32[]{:S(2)}) copy-start(s32[256,4]{0,1:T(4,128)} %param.22) | copy-start | bytes 12292
  286.1 38.4 %copy-start.3 = (bf16[256,4,512]{2,1,0:T(4,128)(2,1)S(1)}, bf16[256,4,512]{2,1,0:T(4,128)(2,1)}, u32[]{:S(2)}) copy-start(bf16[256,4,512]{2,1,0:T(4,128)(2,1)} %param.21) | copy-start | bytes 3145732
  286.1 38.9 %copy-start.12 = (s32[256]{0:T(256)S(1)}, s32[256]{0:T(256)}, u32[]{:S(2)}) copy-start(s32[256]{0:T(256)} %param.23) | copy-start | bytes 3076
  286.1 34.4 %all-to-all-start.1 = ((bf16[3,32,7168]{2,0,1:T(4,128)(2,1)}), bf16[3,32,7168]{2,0,1:T(4,128)(2,1)S(1)}, u32[]{:S(2)}, u32[]{:S(2)}) async-start(bf16[3,32,7168]{2,0,1:T(4,128)(2,1)} %constant_dynamic-slice_fusion), calls=%async_computation.1 | async-start | bytes 3670016 | tf_op jit(solution)/shard_map/all_to_all | solution.py:110
  293.5 125.9 %all-gather.4.cloned.1.call-start = ((), (), s32[]{:S(2)}) async-start(), calls=%async_computation.2 | async-start | bytes 29589504 | tf_op jit(solution)/shard_map/all_gather | solution.py:117
  525.5 61.0 %copy-start.4 = (bf16[256,4,512]{2,1,0:T(4,128)(2,1)S(1)}, bf16[256,4,512]{2,1,0:T(4,128)(2,1)}, u32[]{:S(2)}) copy-start(bf16[256,4,512]{2,1,0:T(4,128)(2,1)} %param.21) | copy-start | bytes 3145732
  525.5 61.0 %copy-start.8 = (s32[256,4]{1,0:T(8,128)S(1)}, s32[256,4]{1,0:T(8,128)}, u32[]{:S(2)}) copy-start(s32[256,4]{1,0:T(8,128)} %copy.78) | copy-start | bytes 12292
  582.6 3.9 copy-start.2
  586.5 68.6 %copy-start.1 = (bf16[7168,32]{0,1:T(8,128)(2,1)S(1)}, bf16[7168,32]{0,1:T(8,128)(2,1)}, u32[]{:S(2)}) copy-start(bf16[7168,32]{0,1:T(8,128)(2,1)} %param.14) | copy-start | bytes 1376260
Sparse Core Ops, SparseCore 0:
  141.0 141.6 all-reduce.14
  323.8 95.5 all-gather.3
